TPU v7x, 256 devices: a whole 4x4x8 slice. The times are simulated.
256 devices in a mesh: replica: 8 (over y, core), fsdp: 32 (over x, z).
Axes of the slice: x: 4, y: 4, z: 8, core: 2. Of those that a mesh axis runs over, the one named last changes fastest.
Arguments:
- anchor_params: bfloat16 [24, 512, 4096], P(None, 'fsdp')
- replica_params: bfloat16 [8, 24, 512, 4096], P('replica', None, 'fsdp')
- projection: bfloat16 [4096, 384], replicated
- momentum: float32 [24, 512, 384], P(None, 'fsdp'), may hold values from -1.8 to 1.8
- rate_table: float32 [4, 6], replicated, may hold values from 0.1 to 1
- owner_list: int32 [24], replicated, may hold values from 0 to 31, as said below
- layer_kind: int32 [24, 2], replicated, may hold values from 0 to 5, as said below
Outputs:
- new_params: bfloat16 [24, 512, 4096], P(None, 'fsdp')
- new_momentum: float32 [24, 512, 384], P(None, 'fsdp')
Inputs may be any that keep to these rules, and one draw needn't show every extreme that they name: `owner_list`: no fsdp index is named more than 2 times, and in every draw some index is named exactly 2 times. `layer_kind`: column 0 is a layer, column 1 a kind below 6; each layer has 6 rows, and no two rows are equal.
All inputs are finite; a program needn't handle non-finite values.
Results may differ from a plain program's by a relative error of at most 0.0055.
Values may be sent and summed in bfloat16 or wider, within the bound.
No kernel may reach another device: no remote copies, remote signals or barrier semaphores. Data moves between devices by JAX's collectives and lax.ppermute only.
A program may use at most 128 MiB of HBM per device.

v0:
```python
import jax
import jax.numpy as jnp
from jax import lax
from jax.sharding import PartitionSpec as P

OUTER_MOMENTUM = 0.9
EPSILON = 1e-06


def decompress(direction, projection):
    flattened = direction.reshape(-1, direction.shape[-1])
    return lax.dot_general(
        flattened, projection, (((1,), (1,)), ((), ())), preferred_element_type=jnp.float32
    ).astype(jnp.bfloat16)


def local(anchor_params, replica_params, projection, momentum, rate_table, owner_list, layer_kind):
    matrices, rows_dev, model_width = anchor_params.shape
    rank_dim = projection.shape[1]
    fsdp_size = lax.axis_size("fsdp")
    own_bound = max(2, (matrices + fsdp_size - 1) // fsdp_size + 1)
    all_rows = rows_dev * fsdp_size
    highest = lax.Precision.HIGHEST
    pseudo_grad = (
        anchor_params.astype(jnp.float32) - replica_params[0].astype(jnp.float32)
    ).astype(jnp.bfloat16)
    compressed = jnp.dot(
        pseudo_grad.reshape(matrices * rows_dev, model_width),
        projection,
        preferred_element_type=jnp.float32,
    )
    summed = lax.psum(compressed.reshape(matrices, rows_dev, rank_dim), "replica")
    outer_grad = summed / lax.axis_size("replica")
    new_momentum = OUTER_MOMENTUM * momentum + outer_grad
    outer_step = outer_grad + OUTER_MOMENTUM * new_momentum
    same_group = (owner_list[:, None] == owner_list[None, :]).astype(jnp.float32)
    layer_onehot = (layer_kind[:, 0:1] == jnp.arange(rate_table.shape[0])[None, :]).astype(
        jnp.float32
    )
    kind_onehot = (layer_kind[:, 1:2] == jnp.arange(rate_table.shape[1])[None, :]).astype(
        jnp.float32
    )
    outer_rate = jnp.sum(jnp.dot(layer_onehot, rate_table, precision=highest) * kind_onehot, axis=1)
    own_index = lax.axis_index("fsdp")
    earlier = jnp.arange(matrices)[:, None] > jnp.arange(matrices)[None, :]
    position = jnp.sum(jnp.where(earlier, same_group, 0.0), axis=1).astype(jnp.int32)
    slot_of = owner_list * own_bound + position
    slot_ids = jnp.arange(fsdp_size * own_bound, dtype=jnp.int32)
    picker = (slot_ids[:, None] == slot_of[None, :]).astype(jnp.float32)
    outgoing = jnp.dot(picker, outer_step.reshape(matrices, -1), precision=highest).reshape(
        fsdp_size, own_bound, rows_dev, rank_dim
    )
    incoming = lax.all_to_all(outgoing, "fsdp", split_axis=0, concat_axis=0, tiled=True)
    own_slots = own_index * own_bound + jnp.arange(own_bound, dtype=jnp.int32)
    owned_slots = (slot_of[None, :] == own_slots[:, None]).astype(jnp.float32)
    owned_count = jnp.maximum(jnp.sum(owned_slots), 1.0)
    group_squares = jnp.sum(incoming * incoming)
    scaling = lax.rsqrt(group_squares / (owned_count * (all_rows * rank_dim)) + EPSILON)
    slot_rate = jnp.dot(owned_slots, outer_rate, precision=highest)
    slot_direction = (incoming * (slot_rate * scaling)[None, :, None, None]).astype(jnp.bfloat16)
    back_picker = picker.T.astype(jnp.bfloat16)
    slot_update = decompress(slot_direction, projection).reshape(
        fsdp_size, own_bound, rows_dev, model_width
    )
    returned = lax.all_to_all(slot_update, "fsdp", split_axis=0, concat_axis=0, tiled=True)
    update = (
        jnp.dot(
            back_picker,
            returned.reshape(fsdp_size * own_bound, -1),
            preferred_element_type=jnp.float32,
        )
        .astype(jnp.bfloat16)
        .reshape(matrices, rows_dev, model_width)
    )
    new_params = (anchor_params.astype(jnp.float32) - update.astype(jnp.float32)).astype(
        jnp.bfloat16
    )
    return (new_params, new_momentum)


def solution(mesh):
    placed = (
        P(None, "fsdp", None),
        P("replica", None, "fsdp", None),
        P(),
        P(None, "fsdp", None),
        P(),
        P(),
        P(),
    )
    return jax.shard_map(
        local,
        mesh=mesh,
        in_specs=placed,
        out_specs=(P(None, "fsdp", None), P(None, "fsdp", None)),
        check_vma=False,
    )
```

profile of v0, /device:TPU:24, one launch (start us, length us, event | category | flops | bytes accessed | tf_op | source)
XLA Modules:
  0.0 368.5 jit_solution(15477138471797277751)
XLA Ops:
  7.2 0.0 copy-start
  7.2 0.0 all-reduce.2.cloned.1.call-start
  7.2 1.8 copy-done
  9.1 5.4 %fusion.3 = f32[24,16,384]{2,1,0:T(8,128)} fusion(bf16[24,16,4096]{2,1,0:T(8,128)(2,1)} %param.7, bf16[1,24,16,4096]{3,2,1,0:T(8,128)(2,1)} %param.8, bf16[4096,384]{1,0:T(8,128)(2,1)S(1)} %copy-done), kind=kOutput, calls=%fused_computation.7 | convolution fusion | flops 1214251008 | bytes 10027008 | tf_op jit(solution)/shard_map/dot_general | solution.py:27
  14.5 0.0 all-reduce.2.cloned.1.call-update
  14.5 0.2 select_reduce_fusion
  14.7 66.8 %all-reduce.2.cloned.1.call-done = f32[24,16,384]{2,1,0:T(8,128)} async-done(((f32[24,16,384]{2,1,0:T(8,128)}), f32[24,16,384]{2,1,0:T(8,128)}) %all-reduce.2.cloned.1.call-update) | async-done | bytes 589840 | tf_op jit(solution)/shard_map/psum | solution.py:32
  81.6 2.2 multiply_add_fusion
  83.7 0.9 fusion.9
  84.6 0.0 copy-start.2
  84.7 2.1 copy.14
  86.7 9.9 %all-to-all-start = ((f32[32,2,16,384]{3,2,1,0:T(8,128)}), f32[32,2,16,384]{3,2,1,0:T(8,128)}, u32[]{:S(2)}, u32[]{:S(2)}) async-start(f32[32,2,16,384]{3,2,1,0:T(8,128)} %copy.14), calls=%async_computation | async-start | bytes 3145728 | tf_op jit(solution)/shard_map/all_to_all | solution.py:53
  96.7 0.7 fusion.18
  98.0 0.2 fusion.7
  98.2 38.5 %all-to-all-done = f32[32,2,16,384]{3,2,1,0:T(8,128)} async-done(((f32[32,2,16,384]{3,2,1,0:T(8,128)}), f32[32,2,16,384]{3,2,1,0:T(8,128)}, u32[]{:S(2)}, u32[]{:S(2)}) %all-to-all-start) | async-done | bytes 1572896 | tf_op jit(solution)/shard_map/all_to_all | solution.py:53
  136.7 2.4 multiply_reduce_fusion
  139.8 0.2 fusion.8
  140.0 1.6 multiply_convert_fusion
  141.6 4.8 %convolution_convert_fusion.1 = bf16[1024,4096]{1,0:T(8,128)(2,1)S(1)} fusion(bf16[1024,384]{1,0:T(8,128)(2,1)S(1)} %bitcast.56, bf16[4096,384]{1,0:T(8,128)(2,1)S(1)} %copy-done), kind=kOutput, calls=%fused_computation.4 | convolution fusion | flops 3225419776 | bytes 12320768 | tf_op jit(solution)/shard_map/dot_general | solution.py:12
  146.4 192.3 %all_to_all.10 = bf16[32,2,16,4096]{3,2,1,0:T(8,128)(2,1)} all-to-all(bf16[32,2,16,4096]{3,2,1,0:T(8,128)(2,1)S(1)} %bitcast.54), channel_id=1, replica_groups=mesh['replica'=8,'fsdp'=32] {'fsdp'}, dimensions={0} | all-to-all | bytes 16777216 | tf_op jit(solution)/shard_map/all_to_all | solution.py:65
  338.8 12.0 %copy.18 = bf16[8,8,16,4096]{3,1,2,0:T(8,128)(2,1)} copy(bf16[8,8,16,4096]{3,2,1,0:T(8,128)(2,1)} %bitcast.52) | data formatting | bytes 16777216
  350.7 4.7 %fusion = f32[24,65536]{1,0:T(8,128)S(1)} fusion(bf16[64,65536]{1,0:T(8,128)(2,1)} %bitcast.51, s32[24]{0:T(128)S(1)} %convert_add_fusion), kind=kOutput, calls=%fused_computation.1 | convolution fusion | flops 204476928 | bytes 14680160 | tf_op jit(solution)/shard_map/dot_general | solution.py:67
  355.4 3.6 copy.19
  359.0 2.6 fusion.2
  (11 shorter events, 0.0 us)
Async XLA Ops:
  7.2 1.9 copy-start
  7.2 7.4 %copy-start.4 = (s32[24]{0:T(128)S(1)}, s32[24]{0:T(128)}, u32[]{:S(2)}) copy-start(s32[24]{0:T(128)} %param.12) | copy-start | bytes 292
  7.2 74.4 %all-reduce.2.cloned.1.call-start = ((), (), s32[]{:S(2)}) async-start(), calls=%async_computation.2 | async-start | bytes 1179648 | tf_op jit(solution)/shard_map/psum | solution.py:32
  84.6 13.3 %copy-start.2 = (s32[24,2]{0,1:T(2,128)S(1)}, s32[24,2]{0,1:T(2,128)}, u32[]{:S(2)}) copy-start(s32[24,2]{0,1:T(2,128)} %param.13) | copy-start | bytes 580
  84.7 13.4 %copy-start.3 = (f32[4,6]{1,0:T(4,128)S(1)}, f32[4,6]{1,0:T(4,128)}, u32[]{:S(2)}) copy-start(f32[4,6]{1,0:T(4,128)} %param.11) | copy-start | bytes 292
  86.7 50.0 %all-to-all-start = ((f32[32,2,16,384]{3,2,1,0:T(8,128)}), f32[32,2,16,384]{3,2,1,0:T(8,128)}, u32[]{:S(2)}, u32[]{:S(2)}) async-start(f32[32,2,16,384]{3,2,1,0:T(8,128)} %copy.14), calls=%async_computation | async-start | bytes 3145728 | tf_op jit(solution)/shard_map/all_to_all | solution.py:53
  355.4 3.7 copy-start.1
Sparse Core Ops, SparseCore 0:
  14.7 66.8 all-reduce.1
where the time goes:
time: 369 us
  blocking collectives  192 us (52%)
  waiting for transfers between devices  105 us (28%)
  local copies, waits for them, and re-layouts  19.5 us (5%)
  matrix products  16.2 us (4%)
  between operations  15.5 us (4%)
  starting transfers between devices  9.97 us (3%)
  other arithmetic  9.73 us (3%)
    all_to_all x1, blocking collectives, local(): lax.all_to_all(slot_update, 'fsdp', split_axis=0, concat_axis=0, tiled=True)  192 us
    psum x1, waiting for transfers between devices, local(): lax.psum(compressed.reshape(matrices, rows_dev, rank_dim), 'replica')  66.8 us
    all_to_all x1, waiting for transfers between devices, local(): lax.all_to_all(outgoing, 'fsdp', split_axis=0, concat_axis=0, tiled=True)  38.5 us
    unnamed x12, local copies, waits for them, and re-layouts  17.5 us
    all_to_all x1, starting transfers between devices, local(): lax.all_to_all(outgoing, 'fsdp', split_axis=0, concat_axis=0, tiled=True)  9.93 us
  transfers between devices with their start and end apart: 2, of which 2 were waited for; matrix products, arithmetic and copies ran while one was open for 0% of the time, Pallas kernels for 0%

commit v1 on v0

--- a/solution.py
+++ b/solution.py
@@ -29,7 +29,9 @@
         projection,
         preferred_element_type=jnp.float32,
     )
-    summed = lax.psum(compressed.reshape(matrices, rows_dev, rank_dim), "replica")
+    summed = jnp.sum(
+        lax.all_gather(compressed.reshape(matrices, rows_dev, rank_dim), "replica"), axis=0
+    )
     outer_grad = summed / lax.axis_size("replica")
     new_momentum = OUTER_MOMENTUM * momentum + outer_grad
     outer_step = outer_grad + OUTER_MOMENTUM * new_momentum

time: 369 us -> 344 us (0.932)
  waiting for transfers between devices: 105 us -> 75.6 us
    psum x1 -> x0, waiting for transfers between devices: 66.8 us -> none  [local(): lax.psum(compressed.reshape(matrices, rows_dev, rank_dim), 'replica')]
    all_gather x0 -> x1, waiting for transfers between devices: none -> 37.6 us  [local(): lax.all_gather(compressed.reshape(matrices, rows_dev, rank_dim), 'replica')]
where the time goes in v1:
time: 344 us; the launch traced here: 341 us
  blocking collectives  191 us (56%)
  waiting for transfers between devices  75.6 us (22%)
  local copies, waits for them, and re-layouts  19.5 us (6%)
  matrix products  16.2 us (5%)
  between operations  15.5 us (5%)
  other arithmetic  13.2 us (4%)
  starting transfers between devices  9.96 us (3%)
    all_to_all x1, blocking collectives, local(): lax.all_to_all(slot_update, 'fsdp', split_axis=0, concat_axis=0, tiled=True)  191 us
    all_to_all x1, waiting for transfers between devices, local(): lax.all_to_all(outgoing, 'fsdp', split_axis=0, concat_axis=0, tiled=True)  38.1 us
    all_gather x1, waiting for transfers between devices, local(): lax.all_gather(compressed.reshape(matrices, rows_dev, rank_dim), 'replica')  37.6 us
    unnamed x12, local copies, waits for them, and re-layouts  17.5 us
    all_to_all x1, starting transfers between devices, local(): lax.all_to_all(outgoing, 'fsdp', split_axis=0, concat_axis=0, tiled=True)  9.92 us
  transfers between devices with their start and end apart: 2, of which 2 were waited for; matrix products, arithmetic and copies ran while one was open for 0% of the time, Pallas kernels for 0%

profile of v1, /device:TPU:24, one launch (start us, length us, event | category | flops | bytes accessed | tf_op | source)
XLA Modules:
  0.0 341.5 jit_solution(5965996344530218006)
XLA Ops:
  7.2 0.0 copy-start
  7.2 0.0 all-gather.3.cloned.1.call-start
  7.2 1.8 copy-done
  9.1 5.4 %fusion.3 = f32[24,16,384]{2,1,0:T(8,128)} fusion(bf16[24,16,4096]{2,1,0:T(8,128)(2,1)} %param.7, bf16[1,24,16,4096]{3,2,1,0:T(8,128)(2,1)} %param.8, bf16[4096,384]{1,0:T(8,128)(2,1)S(1)} %copy-done), kind=kOutput, calls=%fused_computation.7 | convolution fusion | flops 1214251008 | bytes 10027008 | tf_op jit(solution)/shard_map/dot_general | solution.py:27
  14.5 0.0 all-gather.3.cloned.1.call-update
  14.6 0.2 select_reduce_fusion
  14.7 37.6 %all-gather.3.cloned.1.call-done = f32[192,16,384]{2,1,0:T(8,128)} async-done(((f32[24,16,384]{2,1,0:T(8,128)}), f32[192,16,384]{2,1,0:T(8,128)}) %all-gather.3.cloned.1.call-update) | async-done | bytes 4718608 | tf_op jit(solution)/shard_map/all_gather | solution.py:33
  52.3 3.5 %reduce_sum.46 = f32[24,16,384]{2,1,0:T(8,128)} reduce(f32[8,24,16,384]{3,2,1,0:T(8,128)} %bitcast.56, f32[]{:T(128)} %constant.9.clone.1), dimensions={0}, to_apply=%region_1.0 | reduce | flops 1032192 | bytes 5308420 | tf_op jit(solution)/shard_map/reduce_sum | solution.py:32
  55.8 2.2 multiply_add_fusion
  58.0 0.9 fusion.9
  58.9 2.1 copy.14
  61.0 9.9 %all-to-all-start = ((f32[32,2,16,384]{3,2,1,0:T(8,128)}), f32[32,2,16,384]{3,2,1,0:T(8,128)}, u32[]{:S(2)}, u32[]{:S(2)}) async-start(f32[32,2,16,384]{3,2,1,0:T(8,128)} %copy.14), calls=%async_computation | async-start | bytes 3145728 | tf_op jit(solution)/shard_map/all_to_all | solution.py:55
  70.9 0.7 fusion.18
  72.2 0.2 fusion.7
  72.5 38.1 %all-to-all-done = f32[32,2,16,384]{3,2,1,0:T(8,128)} async-done(((f32[32,2,16,384]{3,2,1,0:T(8,128)}), f32[32,2,16,384]{3,2,1,0:T(8,128)}, u32[]{:S(2)}, u32[]{:S(2)}) %all-to-all-start) | async-done | bytes 1572896 | tf_op jit(solution)/shard_map/all_to_all | solution.py:55
  110.5 2.4 multiply_reduce_fusion
  113.7 0.2 fusion.8
  113.8 1.6 multiply_convert_fusion
  115.5 4.8 %convolution_convert_fusion.1 = bf16[1024,4096]{1,0:T(8,128)(2,1)S(1)} fusion(bf16[1024,384]{1,0:T(8,128)(2,1)S(1)} %bitcast.58, bf16[4096,384]{1,0:T(8,128)(2,1)S(1)} %copy-done), kind=kOutput, calls=%fused_computation.4 | convolution fusion | flops 3225419776 | bytes 12320768 | tf_op jit(solution)/shard_map/dot_general | solution.py:12
  120.3 191.4 %all_to_all.10 = bf16[32,2,16,4096]{3,2,1,0:T(8,128)(2,1)} all-to-all(bf16[32,2,16,4096]{3,2,1,0:T(8,128)(2,1)S(1)} %bitcast.55), channel_id=1, replica_groups=mesh['replica'=8,'fsdp'=32] {'fsdp'}, dimensions={0} | all-to-all | bytes 16777216 | tf_op jit(solution)/shard_map/all_to_all | solution.py:67
  311.7 12.0 %copy.18 = bf16[8,8,16,4096]{3,1,2,0:T(8,128)(2,1)} copy(bf16[8,8,16,4096]{3,2,1,0:T(8,128)(2,1)} %bitcast.53) | data formatting | bytes 16777216
  323.7 4.7 %fusion = f32[24,65536]{1,0:T(8,128)S(1)} fusion(bf16[64,65536]{1,0:T(8,128)(2,1)} %bitcast.52, s32[24]{0:T(128)S(1)} %convert_add_fusion), kind=kOutput, calls=%fused_computation.1 | convolution fusion | flops 204476928 | bytes 14680160 | tf_op jit(solution)/shard_map/dot_general | solution.py:69
  328.3 3.6 %copy.19 = f32[3,8,16,4096]{3,2,1,0:T(8,128)S(1)} copy(f32[3,8,16,4096]{3,1,2,0:T(8,128)S(1)} %bitcast.54) | data formatting | bytes 12582912
  332.0 2.6 fusion.2
  (12 shorter events, 0.0 us)
Async XLA Ops:
  7.2 1.9 copy-start
  7.2 7.4 %copy-start.4 = (s32[24]{0:T(128)S(1)}, s32[24]{0:T(128)}, u32[]{:S(2)}) copy-start(s32[24]{0:T(128)} %param.12) | copy-start | bytes 292
  7.2 45.1 %all-gather.3.cloned.1.call-start = ((), (), s32[]{:S(2)}) async-start(), calls=%async_computation.2 | async-start | bytes 5308416 | tf_op jit(solution)/shard_map/all_gather | solution.py:33
  58.9 13.3 %copy-start.2 = (s32[24,2]{0,1:T(2,128)S(1)}, s32[24,2]{0,1:T(2,128)}, u32[]{:S(2)}) copy-start(s32[24,2]{0,1:T(2,128)} %param.13) | copy-start | bytes 580
  58.9 13.3 %copy-start.3 = (f32[4,6]{1,0:T(4,128)S(1)}, f32[4,6]{1,0:T(4,128)}, u32[]{:S(2)}) copy-start(f32[4,6]{1,0:T(4,128)} %param.11) | copy-start | bytes 292
  61.0 49.6 %all-to-all-start = ((f32[32,2,16,384]{3,2,1,0:T(8,128)}), f32[32,2,16,384]{3,2,1,0:T(8,128)}, u32[]{:S(2)}, u32[]{:S(2)}) async-start(f32[32,2,16,384]{3,2,1,0:T(8,128)} %copy.14), calls=%async_computation | async-start | bytes 3145728 | tf_op jit(solution)/shard_map/all_to_all | solution.py:55
  328.3 3.7 %copy-start.1 = (bf16[24,16,4096]{2,1,0:T(8,128)(2,1)S(1)}, bf16[24,16,4096]{2,1,0:T(8,128)(2,1)}, u32[]{:S(2)}) copy-start(bf16[24,16,4096]{2,1,0:T(8,128)(2,1)} %param.7) | copy-start | bytes 9437188
Sparse Core Ops, SparseCore 0:
  14.7 37.5 all-gather.2
